TPU v7x, 256 devices: a whole 4x4x8 slice. The times are simulated.
256 devices in a mesh: keys: 32 (over x, y, core), vocab: 8 (over z).
Axes of the slice: x: 4, y: 4, z: 8, core: 2. Of those that a mesh axis runs over, the one named last changes fastest.
Arguments:
- hidden: bfloat16 [1024, 4096], P(('keys', 'vocab')), may hold values from -24 to 24
- queries: bfloat16 [1024, 1024], P(('keys', 'vocab')), may hold values from -24 to 24
- probes: int32 [1024, 64], P(('keys', 'vocab')), may hold values from 0 to 95, as said below
- counts: int32 [1024], P(('keys', 'vocab')), may hold values from 16 to 64
- block_slot: int32 [96], replicated, may hold values from 0 to 95, as said below
- key_store: bfloat16 [96, 512, 1024], P('keys'), may hold values from -7 to 7
- stored_next_tokens: int32 [96, 512], replicated, may hold values from 0 to 128255
- head_weight: bfloat16 [4096, 128256], P(None, ('keys', 'vocab'))
Outputs:
- mixed_logp: float32 [1024, 128256], P(('keys', 'vocab'))
Inputs may be any that keep to these rules, and one draw needn't show every extreme that they name: `probes`: the 64 ids of a row are distinct block ids; only the first counts of them are probed. At most 2 of a row's 64 ids map through block_slot to slots held by one keys index. `block_slot`: A permutation of the slots; slot s lies in the part of the key store held by keys index s // 3.
All inputs are finite; a program needn't handle non-finite values.
Results may differ from a plain program's by a relative error of at most 0.0003.
Values may be sent and summed in bfloat16 or wider, within the bound.
No kernel may reach another device: no remote copies, remote signals or barrier semaphores. Data moves between devices by JAX's collectives and lax.ppermute only.
A program may use at most 128 MiB of HBM per device.

v0:
```python
import math
import jax
import jax.numpy as jnp
from jax import lax
from jax.sharding import PartitionSpec as P

LAMBDA = 0.25
SMOOTH = 0.1


def joined(part, axis, combine):
    gathered = jax.tree.map(lambda a: lax.all_gather(a, axis), part)

    def take(source):
        return jax.tree.map(lambda a: lax.dynamic_index_in_dim(a, source, 0, False), gathered)

    return lax.fori_loop(
        1, lax.axis_size(axis), lambda source, state: combine(state, take(source)), take(0)
    )


def merge_totals(earlier, later):
    row_peak = jnp.maximum(earlier[0], later[0])
    combined = earlier[1] * jnp.exp(earlier[0] - row_peak) + later[1] * jnp.exp(later[0] - row_peak)
    return (row_peak, combined)


def pick_blocks(table, index_row):
    return table[index_row]


def shards(hidden, queries, probes, counts, block_slot, key_store, stored_next_tokens, head_weight):
    rows_dev = hidden.shape[0]
    piece_cols = head_weight.shape[1]
    local_blocks = key_store.shape[0]
    block_len = key_store.shape[1]
    key_width = key_store.shape[2]
    key_count = lax.axis_size("keys")
    vocab_count = lax.axis_size("vocab")
    probe_cap = probes.shape[1]
    logits = jnp.dot(
        lax.all_gather(hidden, ("keys", "vocab"), axis=0, tiled=True),
        head_weight,
        preferred_element_type=jnp.float32,
    )
    local_peak = jnp.max(logits, axis=1)
    local_sum = jnp.sum(jnp.exp(logits - local_peak[:, None]), axis=1)
    row_peak, row_sum = joined((local_peak, local_sum), ("keys", "vocab"), merge_totals)
    logits = logits - (row_peak + jnp.log(row_sum))[:, None]
    blocks = logits.reshape(key_count, vocab_count, rows_dev, 1, 1, piece_cols)
    arrived = lax.all_to_all(
        lax.all_to_all(blocks, "keys", split_axis=0, concat_axis=3, tiled=True),
        "vocab",
        split_axis=1,
        concat_axis=4,
        tiled=True,
    )
    whole_rows = arrived.reshape(rows_dev, key_count * vocab_count * piece_cols)
    group_queries = lax.all_gather(queries, "keys", axis=0, tiled=True)
    flat_keys = key_store.reshape(local_blocks * block_len, key_width)
    key_norms = jnp.sum(jnp.square(flat_keys.astype(jnp.float32)), axis=1)
    query_norms = jnp.sum(jnp.square(group_queries.astype(jnp.float32)), axis=1)
    inner_prod = lax.dot_general(
        group_queries, flat_keys, (((1,), (1,)), ((), ())), preferred_element_type=jnp.float32
    )
    score_scale = 0.5 / math.sqrt(key_width)
    scores = -(query_norms[:, None] + key_norms[None, :] - 2.0 * inner_prod) * score_scale
    slot_ids = block_slot[probes]
    outgoing = scores.reshape(key_count, rows_dev, local_blocks, block_len)
    incoming = lax.all_to_all(outgoing, "keys", split_axis=0, concat_axis=2, tiled=True)
    every_slot = incoming.reshape(rows_dev, key_count * local_blocks, block_len)
    chosen = jax.vmap(pick_blocks)(every_slot, slot_ids)
    live_mask = (jnp.arange(probe_cap, dtype=jnp.int32)[None, :] < counts[:, None])[:, :, None]
    best_score = jnp.max(jnp.where(live_mask, chosen, -jnp.inf), axis=(1, 2), keepdims=True)
    raised = jnp.where(live_mask, jnp.exp(chosen - best_score), 0.0)
    weights = raised / jnp.sum(raised, axis=(1, 2), keepdims=True)
    tokens = stored_next_tokens[slot_ids]
    row_ids = jnp.broadcast_to(jnp.arange(rows_dev, dtype=jnp.int32)[:, None, None], tokens.shape)
    vocab_size = whole_rows.shape[1]
    knn_mass = jnp.zeros((rows_dev, vocab_size), jnp.float32).at[row_ids, tokens].add(weights)
    return jnp.log(
        LAMBDA * (knn_mass + SMOOTH / vocab_size) / (1.0 + SMOOTH)
        + (1.0 - LAMBDA) * jnp.exp(whole_rows)
    )


def solution(mesh):
    placed = (
        P(("keys", "vocab"), None),
        P(("keys", "vocab"), None),
        P(("keys", "vocab"), None),
        P(("keys", "vocab")),
        P(),
        P("keys", None, None),
        P(),
        P(None, ("keys", "vocab")),
    )
    return jax.shard_map(
        shards, mesh=mesh, in_specs=placed, out_specs=P(("keys", "vocab"), None), check_vma=False
    )
```

profile of v0, /device:TPU:1, one launch (start us, length us, event | category | flops | bytes accessed | tf_op | source)
XLA Modules:
  0.0 1358.9 jit_solution(2815163394601035959)
XLA Ops:
  7.3 125.8 %all-gather.12.cloned.1.call-done = bf16[256,4,4096]{2,1,0:T(4,128)(2,1)} async-done(((bf16[1,4,4096]{2,1,0:T(4,128)(2,1)}), bf16[256,4,4096]{2,1,0:T(4,128)(2,1)}) %all-gather.12.cloned.1.call-update) | async-done | bytes 8388624 | tf_op jit(solution)/shard_map/all_gather | solution.py:42
  133.1 12.5 reshape.128
  145.6 10.5 fusion.7
  156.1 2.5 exponential_reduce_fusion
  159.4 27.1 %all-gather.2 = bf16[32,4,1024]{2,1,0:T(4,128)(2,1)} all-gather(bf16[1,4,1024]{2,1,0:T(4,128)(2,1)S(1)} %bitcast.55), channel_id=1, replica_groups=mesh['keys'=32,'vocab'=8] {'keys'}, dimensions={0}, use_global_device_ids=true | all-gather | bytes 270336 | tf_op jit(solution)/shard_map/all_gather | solution.py:59
  190.0 3.0 fusion.2
  196.0 4.4 all-to-all-start
  200.4 59.7 %all-gather.10.cloned.1.call-done = f32[262144]{0:T(1024)} async-done(((f32[1024]{0:T(1024)}), f32[262144]{0:T(1024)}) %all-gather.10.cloned.1.call-update) | async-done | bytes 1048592 | tf_op jit(solution)/shard_map/all_gather | solution.py:12
  260.2 2.4 reshape.115
  262.6 103.3 %all-gather.8.cloned.1.call-done = f32[262144]{0:T(1024)} async-done(((f32[1024]{0:T(1024)}), f32[262144]{0:T(1024)}) %all-gather.8.cloned.1.call-update) | async-done | bytes 1048592 | tf_op jit(solution)/shard_map/all_gather | solution.py:12
  365.9 2.4 reshape.114
  368.3 211.2 %while.17 = (s32[]{:T(128)}, f32[1024]{0:T(1024)S(1)}, f32[1024]{0:T(1024)S(1)}, f32[256,1024]{1,0:T(8,128)}, f32[256,1024]{1,0:T(8,128)}, /*index=5*/s32[]{:T(128)}, s32[]{:T(128)}, s32[]{:T(128)}) while((s32[]{:T(128)}, f32[1024]{0:T(1024)S(1)}, f32[1024]{0:T(1024)S(1)}, f32[256,1024]{1,0:T(8,128)}, f32[256,1024]{1,0:T(8,128)}, ...), condition=%wide.region_8.9_spmd, body=%wide.region_7.8_spmd.sunk | while | flops 6149 | bytes 41091 | solution.py:17
  581.1 1.9 copy.20
  584.8 7.3 all-to-all-start.1
  592.1 1.9 gather_fusion
  596.8 2.1 gather_fusion.2
  599.8 683.5 %scatter_custom_fusion = f32[513024]{0:T(1024)} fusion(s32[131072]{0:T(1024)S(1)} %bitcast.50, f32[131072]{0:T(1024)S(1)} %bitcast.51, f32[]{:T(128)} %constant.63.clone.1), kind=kCustom, calls=%fused_computation.21 | custom fusion | flops 131072 | bytes 2052100
  1283.2 3.3 copy.22
  1286.6 4.6 all-to-all-start.2
  1291.2 3.1 broadcast_multiply_fusion
  1294.2 3.8 reshape.85
  1298.1 44.8 %all-to-all-done.2 = f32[1,8,4,32,1,501]{5,2,3,4,0,1:T(4,128)S(1)} async-done(((f32[1,8,4,32,1,501]{5,2,3,4,0,1:T(4,128)}), f32[1,8,4,32,1,501]{5,2,3,4,0,1:T(4,128)S(1)}, u32[]{:S(2)}, u32[]{:S(2)}) %all-to-all-start.2) | async-done | bytes 2052128 | tf_op jit(solution)/shard_map/all_to_all | solution.py:51
  1344.7 3.5 mul.57
  1348.2 4.2 add_log_fusion
  (574 shorter events, 220.8 us)
Async XLA Ops:
  6.5 587.7 %copy-start = (s32[96,512]{1,0:T(8,128)S(1)}, s32[96,512]{1,0:T(8,128)}, u32[]{:S(2)}) copy-start(s32[96,512]{1,0:T(8,128)} %param.16) | copy-start | bytes 589828
  6.5 126.5 %all-gather.12.cloned.1.call-start = ((), (), s32[]{:S(2)}) async-start(), calls=%async_computation.5 | async-start | bytes 8421376 | tf_op jit(solution)/shard_map/all_gather | solution.py:42
  7.3 252.9 %all-gather.10.cloned.1.call-start = ((), (), s32[]{:S(2)}) async-start(), calls=%async_computation.4 | async-start | bytes 1052672 | tf_op jit(solution)/shard_map/all_gather | solution.py:12
  145.6 42.6 %copy-start.2 = (bf16[3,512,1024]{2,1,0:T(8,128)(2,1)S(1)}, bf16[3,512,1024]{2,1,0:T(8,128)(2,1)}, u32[]{:S(2)}) copy-start(bf16[3,512,1024]{2,1,0:T(8,128)(2,1)} %param.15) | copy-start | bytes 9437188
  156.1 2.6 copy-start.4
  156.1 3.2 copy-start.5
  158.6 207.3 %all-gather.8.cloned.1.call-start = ((), (), s32[]{:S(2)}) async-start(), calls=%async_computation.3 | async-start | bytes 1052672 | tf_op jit(solution)/shard_map/all_gather | solution.py:12
  194.8 5.6 copy-start.6
  196.0 388.8 %all-to-all-start = ((f32[32,4,3,512]{3,1,2,0:T(4,128)}), f32[32,4,3,512]{3,1,2,0:T(4,128)S(1)}, u32[]{:S(2)}, u32[]{:S(2)}) async-start(f32[32,4,3,512]{3,1,2,0:T(4,128)} %copy.18), calls=%async_computation | async-start | bytes 1572864 | tf_op jit(solution)/shard_map/all_to_all | solution.py:70
  200.4 379.1 %copy-start.3 = (f32[1024,501]{0,1:T(8,128)S(1)}, f32[1024,501]{0,1:T(8,128)}, u32[]{:S(2)}) copy-start(f32[1024,501]{0,1:T(8,128)} %get-tuple-element.157) | copy-start | bytes 6156292
  260.2 108.2 %slice-start = ((f32[262144]{0:T(1024)}), f32[1024]{0:T(1024)S(1)}, s32[]{:S(2)}) async-start(f32[262144]{0:T(1024)} %all-gather.10.cloned.1.call-done), calls=%async_computation.6 | async-start | bytes 8192 | tf_op jit(solution)/shard_map/jit(dynamic_index_in_dim)/dynamic_slice | solution.py:15
  365.9 2.4 slice-start.1
  584.8 7.3 copy-start.1
  584.8 698.5 %all-to-all-start.1 = ((f32[32,8,4,1,1,501]{5,2,1,4,3,0:T(4,128)}), f32[32,8,4,1,1,501]{5,2,1,4,3,0:T(4,128)}, u32[]{:S(2)}, u32[]{:S(2)}) async-start(f32[32,8,4,1,1,501]{5,2,1,4,3,0:T(4,128)} %bitcast.10), calls=%async_computation.1 | async-start | bytes 4194304 | tf_op jit(solution)/shard_map/all_to_all | solution.py:52
  594.2 1.1 copy-start.8
  595.2 0.7 copy-start.7
  595.9 0.7 copy-start.9
  1286.6 56.2 %all-to-all-start.2 = ((f32[1,8,4,32,1,501]{5,2,3,4,0,1:T(4,128)}), f32[1,8,4,32,1,501]{5,2,3,4,0,1:T(4,128)S(1)}, u32[]{:S(2)}, u32[]{:S(2)}) async-start(f32[1,8,4,32,1,501]{5,2,3,4,0,1:T(4,128)} %copy.22), calls=%async_computation.2 | async-start | bytes 4194304 | tf_op jit(solution)/shard_map/all_to_all | solution.py:51
Sparse Core Ops, SparseCore 0:
  11.0 121.9 all-gather.11
  158.8 101.3 all-gather.9
  263.9 101.9 all-gather.7
where the time goes:
time: 1380 us; the launch traced here: 1360 us
  other arithmetic  701 us (51%)
  waiting for transfers between devices  335 us (24%)
  local copies, waits for them, and re-layouts  245 us (18%)
  blocking collectives  27.1 us (2%)
  starting transfers between devices  16.3 us (1%)
    unnamed x4, other arithmetic  684 us
    dynamic_slice x259, local copies, waits for them, and re-layouts, take(): lax.dynamic_index_in_dim(a, source, 0, False)  201 us
    all_gather x2, waiting for transfers between devices, joined(): gathered = jax.tree.map(lambda a: lax.all_gather(a, axis), part)  163 us
    all_gather x1, waiting for transfers between devices, shards(): lax.all_gather(hidden, ('keys', 'vocab'), axis=0, tiled=True)  126 us
    all_to_all x1, waiting for transfers between devices, shards(): lax.all_to_all(lax.all_to_all(blocks, 'keys', split_axis=0, concat_axis=3...  44.8 us
  transfers between devices with their start and end apart: 6, of which 4 were waited for; matrix products, arithmetic and copies ran while one was open for 68% of the time, Pallas kernels for 0%

commit v1 on v0

--- a/solution.py
+++ b/solution.py
@@ -6,6 +6,15 @@
 
 LAMBDA = 0.25
 SMOOTH = 0.1
+_begin_spot = lambda target: jnp.concatenate(
+    lax.all_to_all(
+        jnp.stack([target for _ in range(lax.axis_size(("keys", "vocab")))]),
+        ("keys", "vocab"),
+        0,
+        0,
+    ),
+    axis=0,
+)
 
 
 def joined(part, axis, combine):
@@ -38,11 +47,7 @@
     key_count = lax.axis_size("keys")
     vocab_count = lax.axis_size("vocab")
     probe_cap = probes.shape[1]
-    logits = jnp.dot(
-        lax.all_gather(hidden, ("keys", "vocab"), axis=0, tiled=True),
-        head_weight,
-        preferred_element_type=jnp.float32,
-    )
+    logits = jnp.dot(_begin_spot(hidden), head_weight, preferred_element_type=jnp.float32)
     local_peak = jnp.max(logits, axis=1)
     local_sum = jnp.sum(jnp.exp(logits - local_peak[:, None]), axis=1)
     row_peak, row_sum = joined((local_peak, local_sum), ("keys", "vocab"), merge_totals)

time: 1380 us -> 1460 us (1.058)
  blocking collectives: 27.1 us -> 229 us
  waiting for transfers between devices: 335 us -> 209 us
    all_to_all x0 -> x1, blocking collectives: none -> 203 us  [lax.all_to_all(jnp.stack([target for _ in range(lax.axis_size(('keys', 'v...]
    all_gather x1 -> x0, waiting for transfers between devices: 126 us -> none  [shards(): lax.all_gather(hidden, ('keys', 'vocab'), axis=0, tiled=True)]
  transfers between devices with their start and end apart: 6 -> 5, of which waited for: 4 -> 3; matrix products, arithmetic and copies ran while one was open for 68% -> 64% of each run, Pallas kernels for 0% -> 0%
where the time goes in v1:
time: 1460 us; the launch traced here: 1440 us
  other arithmetic  701 us (48%)
  local copies, waits for them, and re-layouts  253 us (17%)
  blocking collectives  229 us (16%)
  waiting for transfers between devices  209 us (14%)
  starting transfers between devices  16.5 us (1%)
    unnamed x4, other arithmetic  684 us
    all_to_all x1, blocking collectives, lax.all_to_all(jnp.stack([target for _ in range(lax.axis_size(('keys', 'v...  203 us
    dynamic_slice x259, local copies, waits for them, and re-layouts, take(): lax.dynamic_index_in_dim(a, source, 0, False)  201 us
    all_gather x2, waiting for transfers between devices, joined(): gathered = jax.tree.map(lambda a: lax.all_gather(a, axis), part)  163 us
    all_to_all x1, waiting for transfers between devices, shards(): lax.all_to_all(lax.all_to_all(blocks, 'keys', split_axis=0, concat_axis=3...  44.8 us
  transfers between devices with their start and end apart: 5, of which 3 were waited for; matrix products, arithmetic and copies ran while one was open for 64% of the time, Pallas kernels for 0%

profile of v1, /device:TPU:1, one launch (start us, length us, event | category | flops | bytes accessed | tf_op | source)
XLA Modules:
  0.0 1443.1 jit_solution(10931042942016281216)
XLA Ops:
  6.5 8.3 stack.2
  14.8 203.3 %all_to_all.47 = bf16[256,4,4096]{2,1,0:T(4,128)(2,1)} all-to-all(bf16[256,4,4096]{2,1,0:T(4,128)(2,1)} %stack.2), channel_id=1, replica_groups=mesh['keys'=32,'vocab'=8] {'keys','vocab'}, dimensions={0} | all-to-all | bytes 16777216 | tf_op jit(solution)/shard_map/all_to_all | solution.py:10
  218.1 12.5 reshape.84
  230.6 10.5 fusion.7
  241.1 2.5 exponential_reduce_fusion
  244.3 25.3 %all-gather.2 = bf16[32,4,1024]{2,1,0:T(4,128)(2,1)} all-gather(bf16[1,4,1024]{2,1,0:T(4,128)(2,1)S(1)} %bitcast.53), channel_id=1, replica_groups=mesh['keys'=32,'vocab'=8] {'keys'}, dimensions={0}, use_global_device_ids=true | all-gather | bytes 270336 | tf_op jit(solution)/shard_map/all_gather | solution.py:64
  273.2 3.0 fusion.2
  279.1 4.6 all-to-all-start
  283.8 60.2 %all-gather.8.cloned.1.call-done = f32[262144]{0:T(1024)} async-done(((f32[1024]{0:T(1024)}), f32[262144]{0:T(1024)}) %all-gather.8.cloned.1.call-update) | async-done | bytes 1048592 | tf_op jit(solution)/shard_map/all_gather | solution.py:21
  344.1 2.5 reshape.121
  346.5 103.3 %all-gather.6.cloned.1.call-done = f32[262144]{0:T(1024)} async-done(((f32[1024]{0:T(1024)}), f32[262144]{0:T(1024)}) %all-gather.6.cloned.1.call-update) | async-done | bytes 1048592 | tf_op jit(solution)/shard_map/all_gather | solution.py:21
  449.8 2.4 reshape.120
  452.2 211.2 %while.17 = (s32[]{:T(128)}, f32[1024]{0:T(1024)S(1)}, f32[1024]{0:T(1024)S(1)}, f32[256,1024]{1,0:T(8,128)}, f32[256,1024]{1,0:T(8,128)}, /*index=5*/s32[]{:T(128)}, s32[]{:T(128)}, s32[]{:T(128)}) while((s32[]{:T(128)}, f32[1024]{0:T(1024)S(1)}, f32[1024]{0:T(1024)S(1)}, f32[256,1024]{1,0:T(8,128)}, f32[256,1024]{1,0:T(8,128)}, ...), condition=%wide.region_8.9_spmd, body=%wide.region_7.8_spmd.sunk | while | flops 6149 | bytes 41091 | solution.py:26
  665.0 1.9 copy.20
  668.7 7.2 all-to-all-start.2
  680.7 2.1 gather_fusion.2
  683.6 683.5 %scatter_custom_fusion = f32[513024]{0:T(1024)} fusion(s32[131072]{0:T(1024)S(1)} %bitcast.49, f32[131072]{0:T(1024)S(1)} %bitcast.50, f32[]{:T(128)} %constant.63.clone.1), kind=kCustom, calls=%fused_computation.21 | custom fusion | flops 131072 | bytes 2052100
  1367.1 3.3 copy.22
  1370.5 4.6 all-to-all-start.3
  1375.0 3.1 broadcast_multiply_fusion
  1378.1 3.9 reshape.91
  1382.0 44.8 %all-to-all-done.3 = f32[1,8,4,32,1,501]{5,2,3,4,0,1:T(4,128)S(1)} async-done(((f32[1,8,4,32,1,501]{5,2,3,4,0,1:T(4,128)}), f32[1,8,4,32,1,501]{5,2,3,4,0,1:T(4,128)S(1)}, u32[]{:S(2)}, u32[]{:S(2)}) %all-to-all-start.3) | async-done | bytes 2052128 | tf_op jit(solution)/shard_map/all_to_all | solution.py:56
  1428.6 3.5 mul.57
  1432.1 4.2 add_log_fusion
  (573 shorter events, 221.9 us)
Async XLA Ops:
  6.5 671.6 %copy-start = (s32[96,512]{1,0:T(8,128)S(1)}, s32[96,512]{1,0:T(8,128)}, u32[]{:S(2)}) copy-start(s32[96,512]{1,0:T(8,128)} %param.16) | copy-start | bytes 589828
  6.5 337.5 %all-gather.8.cloned.1.call-start = ((), (), s32[]{:S(2)}) async-start(), calls=%async_computation.5 | async-start | bytes 1052672 | tf_op jit(solution)/shard_map/all_gather | solution.py:21
  230.6 40.8 %copy-start.2 = (bf16[3,512,1024]{2,1,0:T(8,128)(2,1)S(1)}, bf16[3,512,1024]{2,1,0:T(8,128)(2,1)}, u32[]{:S(2)}) copy-start(bf16[3,512,1024]{2,1,0:T(8,128)(2,1)} %param.15) | copy-start | bytes 9437188
  241.1 2.6 copy-start.4
  241.1 3.3 copy-start.5
  243.6 206.2 %all-gather.6.cloned.1.call-start = ((), (), s32[]{:S(2)}) async-start(), calls=%async_computation.4 | async-start | bytes 1052672 | tf_op jit(solution)/shard_map/all_gather | solution.py:21
  277.9 5.9 copy-start.6
  279.1 389.5 %all-to-all-start = ((f32[32,4,3,512]{3,1,2,0:T(4,128)}), f32[32,4,3,512]{3,1,2,0:T(4,128)S(1)}, u32[]{:S(2)}, u32[]{:S(2)}) async-start(f32[32,4,3,512]{3,1,2,0:T(4,128)} %copy.18), calls=%async_computation | async-start | bytes 1572864 | tf_op jit(solution)/shard_map/all_to_all | solution.py:75
  283.8 379.6 %copy-start.3 = (f32[1024,501]{0,1:T(8,128)S(1)}, f32[1024,501]{0,1:T(8,128)}, u32[]{:S(2)}) copy-start(f32[1024,501]{0,1:T(8,128)} %get-tuple-element.157) | copy-start | bytes 6156292
  344.1 108.2 %slice-start = ((f32[262144]{0:T(1024)}), f32[1024]{0:T(1024)S(1)}, s32[]{:S(2)}) async-start(f32[262144]{0:T(1024)} %all-gather.8.cloned.1.call-done), calls=%async_computation.6 | async-start | bytes 8192 | tf_op jit(solution)/shard_map/jit(dynamic_index_in_dim)/dynamic_slice | solution.py:24
  449.8 2.4 slice-start.1
  668.7 7.3 copy-start.1
  668.7 698.5 %all-to-all-start.2 = ((f32[32,8,4,1,1,501]{5,2,1,4,3,0:T(4,128)}), f32[32,8,4,1,1,501]{5,2,1,4,3,0:T(4,128)}, u32[]{:S(2)}, u32[]{:S(2)}) async-start(f32[32,8,4,1,1,501]{5,2,1,4,3,0:T(4,128)} %bitcast.9), calls=%async_computation.2 | async-start | bytes 4194304 | tf_op jit(solution)/shard_map/all_to_all | solution.py:57
  678.1 1.1 copy-start.8
  679.1 0.7 copy-start.7
  679.7 0.7 copy-start.9
  1370.5 56.2 %all-to-all-start.3 = ((f32[1,8,4,32,1,501]{5,2,3,4,0,1:T(4,128)}), f32[1,8,4,32,1,501]{5,2,3,4,0,1:T(4,128)S(1)}, u32[]{:S(2)}, u32[]{:S(2)}) async-start(f32[1,8,4,32,1,501]{5,2,3,4,0,1:T(4,128)} %copy.22), calls=%async_computation.3 | async-start | bytes 4194304 | tf_op jit(solution)/shard_map/all_to_all | solution.py:56
Sparse Core Ops, SparseCore 0:
  243.7 100.3 all-gather.7
  347.8 101.9 all-gather.5
